TPU v7x, 32 devices: a whole 2x2x4 slice. The times are simulated.
32 devices in a mesh: layer: 4 (over x, core), tok: 8 (over z, y).
Axes of the slice: x: 2, y: 2, z: 4, core: 2. Of those that a mesh axis runs over, the one named last changes fastest.
Arguments:
- active_codes: bfloat16 [4, 1024, 32], P('layer', 'tok'), may hold values from 0.19921875 to 3
- latent_ids: int32 [4, 1024, 32], P('layer', 'tok'), may hold values from 0 to 32767, as said below
- decoder: bfloat16 [4, 32768, 4096], P('layer', 'tok'), may hold values from -1 to 1
- carry_gain: float32 [4, 4096], P('layer'), may hold values from 0.1 to 1
- earlier_sum: bfloat16 [1024, 4096], P('tok'), may hold values from -6 to 6
- targets: bfloat16 [4, 1024, 4096], P('layer', 'tok'), may hold values from -6 to 6
Outputs:
- reconstruction: bfloat16 [4, 1024, 4096], P('layer', 'tok')
- code_grad: float32 [4, 1024, 32], P('layer', 'tok')
Inputs may be any that keep to these rules, and one draw needn't show every extreme that they name: `latent_ids`: A token's 32 ids in one layer are distinct. In each layer, the 128 tokens of one aligned block have at most 768 ids in any one range of 4096 consecutive latents, and in every layer one range holds exactly 768 ids of every block.
All inputs are finite; a program needn't handle non-finite values.
Results may differ from a plain program's by a relative error of at most 0.019.
Values may be sent and summed in bfloat16 or wider, within the bound.
No kernel may reach another device: no remote copies, remote signals or barrier semaphores. Data moves between devices by JAX's collectives and lax.ppermute only.
A program may use at most 256 MiB of HBM per device.

v0:
```python
import jax
import jax.numpy as jnp
from jax import lax
from jax.sharding import PartitionSpec as P


def prefix(shard, axis, combine, identity, reverse):
    length, mine = (lax.axis_size(axis), lax.axis_index(axis))
    everything = jax.tree.map(
        lambda part, kind: lax.all_gather(part.astype(kind), axis),
        shard,
        (jnp.bfloat16, jnp.bfloat16),
    )
    start = jax.tree.map(
        lambda part, zero: jnp.broadcast_to(jnp.asarray(zero, part.dtype), part.shape),
        shard,
        identity,
    )

    def lap(k, before):
        at = length - 1 - k if reverse else k
        reached = at > mine if reverse else at < mine
        new = combine(
            before, jax.tree.map(lambda part, own: part[at].astype(own.dtype), everything, shard)
        )
        return jax.tree.map(lambda a, b: jnp.where(reached, a, b), new, before)

    return lax.fori_loop(0, length, lap, start)


def bucket_lists(latent_rows, code_rows, range_size, owners, capacity):
    tok_rows, top_count = latent_rows.shape
    entries = tok_rows * top_count
    flat_ids = latent_rows.reshape(entries)
    owning = flat_ids // range_size
    within = flat_ids % range_size
    positions = jnp.arange(entries, dtype=jnp.int32) // top_count
    ordering = jnp.argsort(owning, stable=True)
    counts = jnp.sum(
        (owning[:, None] == jnp.arange(owners, dtype=jnp.int32)[None, :]).astype(jnp.int32), axis=0
    )
    starts = jnp.cumsum(counts) - counts
    sorted_rank = jnp.arange(entries, dtype=jnp.int32) - starts[owning[ordering]]
    rank_of = jnp.zeros(entries, jnp.int32).at[ordering].set(sorted_rank)
    slot_index = owning * capacity + rank_of
    slot_keys = (
        jnp.zeros(owners * capacity, jnp.int32).at[slot_index].set(within * tok_rows + positions)
    )
    slot_codes = (
        jnp.zeros(owners * capacity, jnp.bfloat16).at[slot_index].set(code_rows.reshape(entries))
    )
    return (slot_keys.reshape(owners, capacity), slot_codes.reshape(owners, capacity), slot_index)


def source_term(rows, slot_keys, slot_codes, tok_rows):
    token_index = slot_keys % tok_rows
    matches = token_index[None, :] == jnp.arange(tok_rows, dtype=jnp.int32)[:, None]
    spread = jnp.where(matches, slot_codes[None, :], jnp.zeros((), jnp.bfloat16))
    return jnp.dot(spread, rows, preferred_element_type=jnp.float32)


def slot_grads_of(rows, slot_keys, grad_block, tok_rows):
    token_index = slot_keys % tok_rows
    products = jnp.einsum("td,cd->tc", grad_block, rows, preferred_element_type=jnp.float32)
    matches = token_index[None, :] == jnp.arange(tok_rows, dtype=jnp.int32)[:, None]
    return jnp.sum(jnp.where(matches, products, 0.0), axis=0)


def compose(earlier_part, later_part):
    return (earlier_part[0] * later_part[0], later_part[0] * earlier_part[1] + later_part[1])


def on_device(active_codes, latent_ids, decoder, carry_gain, earlier_sum, targets):
    owners = lax.axis_size("tok")
    tok_rows = active_codes.shape[1]
    top_count = active_codes.shape[2]
    range_size = decoder.shape[1]
    model_width = decoder.shape[2]
    capacity = 3 * tok_rows * top_count // (2 * owners)
    weights = decoder[0]
    slot_keys, slot_codes, slot_index = bucket_lists(
        latent_ids[0], active_codes[0], range_size, owners, capacity
    )
    recv_keys, recv_codes = (
        lax.all_to_all(slot_keys, "tok", split_axis=0, concat_axis=0, tiled=True),
        lax.all_to_all(slot_codes, "tok", split_axis=0, concat_axis=0, tiled=True),
    )
    row_cache = jnp.take(weights, recv_keys // tok_rows, axis=0)

    def one_source(triple):
        return source_term(triple[2], triple[0], triple[1], tok_rows)

    keys_part = recv_keys
    rows_part = row_cache
    term_blocks = lax.map(one_source, (keys_part, recv_codes, rows_part))
    decoded = lax.psum_scatter(
        term_blocks.reshape(lax.axis_size("tok") * tok_rows, model_width).astype(jnp.bfloat16),
        "tok",
        scatter_dimension=0,
        tiled=True,
    ).astype(jnp.float32)
    identity = (jnp.ones_like(carry_gain), jnp.zeros_like(decoded))
    ahead_gain, ahead_sum = prefix((carry_gain, decoded), "layer", compose, identity, False)
    recon_full = carry_gain * (ahead_gain * earlier_sum.astype(jnp.float32) + ahead_sum) + decoded
    misfit = recon_full - targets[0].astype(jnp.float32)
    behind_gain, behind_sum = prefix(
        (carry_gain, carry_gain * misfit), "layer", compose, identity, True
    )
    grad_low = (misfit + behind_sum).astype(jnp.bfloat16)

    def grads_of_source(triple):
        return slot_grads_of(triple[2], triple[0], triple[1], tok_rows)

    segment = lax.all_gather(grad_low, "tok", axis=0, tiled=True)
    source_count = segment.shape[0] // tok_rows
    keys_part = recv_keys
    rows_part = row_cache
    grad_blocks = segment.reshape(source_count, tok_rows, model_width)
    values = lax.map(grads_of_source, (keys_part, grad_blocks, rows_part))
    returned = lax.all_to_all(values, "tok", split_axis=0, concat_axis=0, tiled=True)
    code_grad = jnp.take(returned.reshape(owners * capacity), slot_index).reshape(
        tok_rows, top_count
    )
    return (recon_full.astype(jnp.bfloat16)[None], code_grad[None])


def solution(mesh):
    return jax.shard_map(
        on_device,
        mesh=mesh,
        in_specs=(
            P("layer", "tok", None),
            P("layer", "tok", None),
            P("layer", "tok", None),
            P("layer", None),
            P("tok", None),
            P("layer", "tok", None),
        ),
        out_specs=(P("layer", "tok", None), P("layer", "tok", None)),
        check_vma=False,
    )
```

profile of v0, /device:TPU:0, one launch (start us, length us, event | category | flops | bytes accessed | tf_op | source)
XLA Modules:
  0.0 932.6 jit_solution(17020449953633308792)
XLA Ops:
  9.1 5.8 sort.17
  14.9 23.0 %gather_fusion = s32[4096]{0:T(1024)S(1)} fusion(s32[4096]{0:T(1024)S(1)} %add_select_fusion.3, s32[4096]{0:T(1024)S(1)} %get-tuple-element.481), kind=kCustom, calls=%fused_computation | custom fusion | bytes 49152 | tf_op jit(solution)/shard_map/gather | solution.py:43
  43.0 15.5 %scatter_custom_fusion = s32[4096]{0:T(1024)S(1)} fusion(s32[4096]{0:T(1024)S(1)} %get-tuple-element.482, s32[4096]{0:T(1024)S(1)} %select_subtract_fusion, s32[]{:T(128)} %constant.237.clone.1), kind=kCustom, calls=%fused_computation.106 | custom fusion | bytes 16388 | tf_op jit(solution)/shard_map/scatter | solution.py:44
  59.4 28.6 %scatter_custom_fusion.2 = bf16[6144]{0:T(1024)(128)(2,1)S(1)} fusion(s32[4096]{0:T(1024)S(1)} %get-tuple-element.475, bf16[4096]{0:T(1024)(128)(2,1)S(1)} %reshape.307, bf16[]{:T(256)} %constant.252.clone.1), kind=kCustom, calls=%fused_computation.108 | custom fusion | bytes 12290 | tf_op jit(solution)/shard_map/scatter | solution.py:50
  89.9 7.3 all-to-all-start.1
  97.1 16.1 %scatter_custom_fusion.1 = s32[6144]{0:T(1024)} fusion(s32[4096]{0:T(1024)S(1)} %get-tuple-element.475, s32[4096]{0:T(1024)S(1)} %get-tuple-element.480, s32[]{:T(128)} %constant.237.clone.1), kind=kCustom, calls=%fused_computation.101 | custom fusion | bytes 24580 | tf_op jit(solution)/shard_map/scatter | solution.py:47
  113.2 6.0 all-to-all-start
  120.1 5.8 all-to-all-done
  126.0 262.2 %gather_fusion.1 = bf16[6144,4096]{1,0:T(8,128)(2,1)} fusion(bf16[4096,4096]{1,0:T(8,128)(2,1)} %bitcast.100, s32[6144]{0:T(1024)S(1)} %broadcast_clamp_fusion), kind=kCustom, calls=%fused_computation.1 | custom fusion | bytes 100687872 | tf_op jit(solution)/shard_map/jit(_take)/gather | solution.py:88
  388.3 33.4 %broadcast_select_fusion.2 = bf16[8,768,4096]{2,1,0:T(8,128)(2,1)} fusion(bf16[8,768,4096]{2,1,0:T(8,128)(2,1)} %bitcast.101, pred[8,768]{1,0:T(8,128)(4,1)S(1)} %compare_and_fusion), kind=kLoop, calls=%fused_computation.46 | loop fusion | flops 25165824 | bytes 100669440 | tf_op jit(solution)/shard_map/jit(_take)/select_n | solution.py:88
  421.7 44.3 %while.56 = (s32[]{:T(128)}, bf16[8,128,4096]{2,1,0:T(8,128)(2,1)}, s32[8,768]{1,0:T(8,128)S(1)}, bf16[8,768]{1,0:T(8,128)(2,1)}, bf16[8,768,4096]{2,1,0:T(8,128)(2,1)}, /*index=5*/s32[]{:T(128)}) while((s32[]{:T(128)}, bf16[8,128,4096]{2,1,0:T(8,128)(2,1)}, s32[8,768]{1,0:T(8,128)S(1)}, bf16[8,768]{1,0:T(8,128)(2,1)}, ...), condition=%wide.region_7.8_spmd, body=%wide.region_6.7_spmd.sunk | while | flops 805511424 | bytes 8403533 | solution.py:95
  433.5 4.8 fusion.63
  450.1 4.8 fusion.63
  461.2 4.8 fusion.63
  466.0 159.1 %reduce-scatter.2.cloned.1.call-done = bf16[128,4096]{1,0:T(8,128)(2,1)} async-done(((bf16[1024,4096]{1,0:T(8,128)(2,1)}), bf16[128,4096]{1,0:T(8,128)(2,1)}) %reduce-scatter.2.cloned.1.call-update) | async-done | bytes 1048592 | tf_op jit(solution)/shard_map/reduce_scatter | solution.py:96
  625.2 5.2 all-gather.3
  630.5 29.8 %all-gather.10.cloned.1.call-done = bf16[512,4096]{1,0:T(8,128)(2,1)} async-done(((bf16[128,4096]{1,0:T(8,128)(2,1)}), bf16[512,4096]{1,0:T(8,128)(2,1)}) %all-gather.10.cloned.1.call-update) | async-done | bytes 4194320 | tf_op jit(solution)/shard_map/all_gather | solution.py:10
  660.2 10.5 %while.58 = (s32[]{:T(128)}, f32[1,4096]{1,0:T(1,128)S(1)}, f32[128,4096]{1,0:T(8,128)S(1)}, s32[]{:T(128)}, bf16[4,1,4096]{2,1,0:T(2,128)(2,1)S(1)}, /*index=5*/bf16[4,128,4096]{2,1,0:T(8,128)(2,1)}, s32[]{:T(128)}, s32[]{:T(128)}) while((s32[]{:T(128)}, f32[1,4096]{1,0:T(1,128)S(1)}, f32[128,4096]{1,0:T(8,128)S(1)}, ...), condition=%wide.region_10.11_spmd.clone, body=%wide.region_9.10_spmd.clone.sunk | while | flops 2637828 | bytes 5316723 | solution.py:28
  674.8 34.6 %all-gather.12.cloned.1.call-done = bf16[512,4096]{1,0:T(8,128)(2,1)} async-done(((bf16[128,4096]{1,0:T(8,128)(2,1)}), bf16[512,4096]{1,0:T(8,128)(2,1)}) %all-gather.12.cloned.1.call-update) | async-done | bytes 4194320 | tf_op jit(solution)/shard_map/all_gather | solution.py:10
  709.3 10.4 %while.59 = (s32[]{:T(128)}, f32[128,4096]{1,0:T(8,128)S(1)}, s32[]{:T(128)}, bf16[4,1,4096]{2,1,0:T(2,128)(2,1)S(1)}, bf16[4,128,4096]{2,1,0:T(8,128)(2,1)}, /*index=5*/s32[]{:T(128)}, s32[]{:T(128)}, s32[]{:T(128)}, s32[]{:T(128)}) while((s32[]{:T(128)}, f32[128,4096]{1,0:T(8,128)S(1)}, s32[]{:T(128)}, ...), condition=%wide.region_12.13_spmd.clone, body=%wide.region_11.12_spmd.clone.sunk | while | flops 2625544 | bytes 5284007 | solution.py:28
  723.9 125.1 %all-gather.8.cloned.1.call-done = bf16[1024,4096]{1,0:T(8,128)(2,1)} async-done(((bf16[128,4096]{1,0:T(8,128)(2,1)}), bf16[1024,4096]{1,0:T(8,128)(2,1)}) %all-gather.8.cloned.1.call-update) | async-done | bytes 8388624 | tf_op jit(solution)/shard_map/all_gather | solution.py:114
  849.0 44.0 %while.57 = (s32[]{:T(128)}, f32[8,768]{1,0:T(8,128)S(1)}, s32[8,768]{1,0:T(8,128)S(1)}, bf16[8,128,4096]{2,1,0:T(8,128)(2,1)}, bf16[8,768,4096]{2,1,0:T(8,128)(2,1)}, /*index=5*/s32[]{:T(128)}, s32[]{:T(128)}) while((s32[]{:T(128)}, f32[8,768]{1,0:T(8,128)S(1)}, s32[8,768]{1,0:T(8,128)S(1)}, bf16[8,128,4096]{2,1,0:T(8,128)(2,1)}, ...), condition=%wide.region_15.16_spmd, body=%wide.region_13.15_spmd.sunk | while | flops 805608960 | bytes 7365717 | solution.py:119
  849.0 5.3 fusion.67
  854.5 5.3 fusion.67
  860.0 5.3 fusion.67
  865.5 5.3 fusion.67
  871.0 5.3 fusion.67
  876.5 5.3 fusion.67
  882.0 5.3 fusion.67
  887.6 5.3 fusion.67
  893.0 9.2 all_to_all.37
  902.3 23.0 %gather_fusion.2 = f32[4096]{0:T(1024)S(1)} fusion(f32[6144]{0:T(1024)S(1)} %bitcast.99, s32[4096]{0:T(1024)S(1)} %copy-done.4), kind=kCustom, calls=%fused_computation.2 | custom fusion | bytes 49152 | tf_op jit(solution)/shard_map/jit(_take)/gather | solution.py:121
  (119 shorter events, 71.2 us)
Async XLA Ops:
  14.9 44.3 %copy-start.5 = (bf16[1,128,32]{1,2,0:T(8,128)(2,1)S(1)}, bf16[1,128,32]{1,2,0:T(8,128)(2,1)}, u32[]{:S(2)}) copy-start(bf16[1,128,32]{1,2,0:T(8,128)(2,1)} %param.14) | copy-start | bytes 24580
  59.2 60.3 %copy-start.2 = (s32[4096]{0:T(1024)}, s32[4096]{0:T(1024)S(1)}, u32[]{:S(2)}) copy-start(s32[4096]{0:T(1024)S(1)} %get-tuple-element.475) | copy-start | bytes 49156
  89.9 23.4 %all-to-all-start.1 = ((bf16[8,2,384]{2,1,0:T(2,128)(2,1)}), bf16[8,2,384]{2,1,0:T(2,128)(2,1)S(1)}, u32[]{:S(2)}, u32[]{:S(2)}) async-start(bf16[8,2,384]{2,1,0:T(2,128)(2,1)} %reshape.367), calls=%async_computation.1 | async-start | bytes 24576 | tf_op jit(solution)/shard_map/all_to_all | solution.py:86
  113.2 12.6 %all-to-all-start = ((s32[8,1,768]{2,1,0:T(1,128)}), s32[8,1,768]{2,1,0:T(1,128)S(1)}, u32[]{:S(2)}, u32[]{:S(2)}) async-start(s32[8,1,768]{2,1,0:T(1,128)} %bitcast.18), calls=%async_computation | async-start | bytes 49152 | tf_op jit(solution)/shard_map/all_to_all | solution.py:85
  119.2 505.9 %reduce-scatter.2.cloned.1.call-start = ((), (), s32[]{:S(2)}) async-start(), calls=%async_computation.4 | async-start | bytes 9437184 | tf_op jit(solution)/shard_map/reduce_scatter | solution.py:96
  466.0 159.2 %copy-start.1 = (f32[1,4096]{1,0:T(1,128)S(1)}, f32[1,4096]{1,0:T(1,128)}, u32[]{:S(2)}) copy-start(f32[1,4096]{1,0:T(1,128)} %param.17) | copy-start | bytes 49156
  466.0 194.3 %all-gather.10.cloned.1.call-start = ((), (), s32[]{:S(2)}) async-start(), calls=%async_computation.6 | async-start | bytes 5242880 | tf_op jit(solution)/shard_map/all_gather | solution.py:10
  625.1 84.2 %all-gather.12.cloned.1.call-start = ((), (), s32[]{:S(2)}) async-start(), calls=%async_computation.7 | async-start | bytes 5242880 | tf_op jit(solution)/shard_map/all_gather | solution.py:10
  660.2 10.6 %copy-start = (bf16[1,128,4096]{2,1,0:T(8,128)(2,1)S(1)}, bf16[1,128,4096]{2,1,0:T(8,128)(2,1)}, u32[]{:S(2)}) copy-start(bf16[1,128,4096]{2,1,0:T(8,128)(2,1)} %param.19) | copy-start | bytes 3145732
  674.7 174.3 %all-gather.8.cloned.1.call-start = ((), (), s32[]{:S(2)}) async-start(), calls=%async_computation.5 | async-start | bytes 9437184 | tf_op jit(solution)/shard_map/all_gather | solution.py:114
  849.0 53.3 %copy-start.4 = (s32[4096]{0:T(1024)S(1)}, s32[4096]{0:T(1024)}, u32[]{:S(2)}) copy-start(s32[4096]{0:T(1024)} %get-tuple-element.474) | copy-start | bytes 49156
  902.3 23.0 %copy-start.3 = (s32[4096]{0:T(1024)S(1)}, s32[4096]{0:T(1024)}, u32[]{:S(2)}) copy-start(s32[4096]{0:T(1024)} %copy-done.2) | copy-start | bytes 49156
Sparse Core Ops, SparseCore 0:
  466.1 158.9 reduce-scatter.1
  626.7 33.4 all-gather.9
  674.8 34.4 all-gather.11
  724.0 124.9 all-gather.7
where the time goes:
time: 940 us; the launch traced here: 933 us
  local copies, waits for them, and re-layouts  379 us (40%)
  waiting for transfers between devices  354 us (38%)
  matrix products  80.9 us (9%)
  other arithmetic  75.3 us (8%)
  blocking collectives  14.5 us (2%)
  between operations  14 us (1%)
  starting transfers between devices  13.6 us (1%)
    gather x1, local copies, waits for them, and re-layouts, on_device(): row_cache = jnp.take(weights, recv_keys // tok_rows, axis=0)  262 us
    reduce_scatter x1, waiting for transfers between devices, on_device(): lax.psum_scatter(term_blocks.reshape(lax.axis_size('tok') * tok_rows, mod...  159 us
    all_gather x1, waiting for transfers between devices, on_device(): segment = lax.all_gather(grad_low, 'tok', axis=0, tiled=True)  125 us
    all_gather x2, waiting for transfers between devices, prefix(): lax.all_gather(part.astype(kind), axis)  64.4 us
    dot_general x8, matrix products, slot_grads_of(): jnp.einsum('td,cd->tc', grad_block, rows, preferred_element_type=jnp.floa...  42.8 us
    dot_general x8, matrix products, source_term(): return jnp.dot(spread, rows, preferred_element_type=jnp.float32)  38.1 us
    select_n x2, other arithmetic, on_device(): row_cache = jnp.take(weights, recv_keys // tok_rows, axis=0)  33.5 us
    scatter x1, local copies, waits for them, and re-layouts, bucket_lists(): jnp.zeros(owners * capacity, jnp.bfloat16).at[slot_index]  28.6 us
  transfers between devices with their start and end apart: 6, of which 5 were waited for; matrix products, arithmetic and copies ran while one was open for 2% of the time, Pallas kernels for 0%

commit v1 on v0

--- a/solution.py
+++ b/solution.py
@@ -2,6 +2,22 @@
 import jax.numpy as jnp
 from jax import lax
 from jax.sharding import PartitionSpec as P
+
+
+def ring_gather(x, axis, dim):
+    ways, here, lap = (lax.axis_size(axis), lax.axis_index(axis), x.shape[dim])
+    lengths = [n * ways if d == dim else n for d, n in enumerate(x.shape)]
+    full = lax.dynamic_update_slice_in_dim(jnp.zeros(lengths, x.dtype), x, here * lap, axis=dim)
+    going_up = going_down = x
+    for far in range(1, ways // 2 + 1):
+        going_up = lax.ppermute(going_up, axis, [(d, (d + 1) % ways) for d in range(ways)])
+        full = lax.dynamic_update_slice_in_dim(full, going_up, (here - far) % ways * lap, axis=dim)
+        if 2 * far < ways:
+            going_down = lax.ppermute(going_down, axis, [(d, (d - 1) % ways) for d in range(ways)])
+            full = lax.dynamic_update_slice_in_dim(
+                full, going_down, (here + far) % ways * lap, axis=dim
+            )
+    return full
 
 
 def prefix(shard, axis, combine, identity, reverse):
@@ -111,7 +127,7 @@
     def grads_of_source(triple):
         return slot_grads_of(triple[2], triple[0], triple[1], tok_rows)
 
-    segment = lax.all_gather(grad_low, "tok", axis=0, tiled=True)
+    segment = ring_gather(grad_low, "tok", 0)
     source_count = segment.shape[0] // tok_rows
     keys_part = recv_keys
     rows_part = row_cache

time: 940 us -> 985 us (1.048)
  waiting for transfers between devices: 354 us -> 376 us
  starting transfers between devices: 13.6 us -> 34.6 us
  local copies, waits for them, and re-layouts: 379 us -> 394 us
    ppermute x0 -> x7, waiting for transfers between devices: none -> 141 us  [the longest x4 141 us: ring_gather(): lax.ppermute(going_up, axis, [(d, (d + 1) % ways) for d in range(ways)])]
    all_gather x1 -> x0, waiting for transfers between devices: 125 us -> none  [on_device(): segment = lax.all_gather(grad_low, 'tok', axis=0, tiled=True)]
    ppermute x0 -> x7, starting transfers between devices: none -> 17.7 us  [the longest x4 8.92 us: ring_gather(): lax.ppermute(going_up, axis, [(d, (d + 1) % ways) for d in range(ways)])]
  transfers between devices with their start and end apart: 6 -> 13, of which waited for: 5 -> 9; matrix products, arithmetic and copies ran while one was open for 2% -> 3% of each run, Pallas kernels for 0% -> 0%
where the time goes in v1:
time: 985 us; the launch traced here: 978 us
  local copies, waits for them, and re-layouts  394 us (40%)
  waiting for transfers between devices  376 us (38%)
  matrix products  81 us (8%)
  other arithmetic  72.8 us (7%)
  starting transfers between devices  34.6 us (4%)
  between operations  14 us (1%)
    gather x1, local copies, waits for them, and re-layouts, on_device(): row_cache = jnp.take(weights, recv_keys // tok_rows, axis=0)  262 us
    reduce_scatter x1, waiting for transfers between devices, on_device(): lax.psum_scatter(term_blocks.reshape(lax.axis_size('tok') * tok_rows, mod...  159 us
    ppermute x4, waiting for transfers between devices, ring_gather(): lax.ppermute(going_up, axis, [(d, (d + 1) % ways) for d in range(ways)])  141 us
    all_gather x2, waiting for transfers between devices, prefix(): lax.all_gather(part.astype(kind), axis)  64.4 us
    dot_general x8, matrix products, slot_grads_of(): jnp.einsum('td,cd->tc', grad_block, rows, preferred_element_type=jnp.floa...  42.9 us
    dot_general x8, matrix products, source_term(): return jnp.dot(spread, rows, preferred_element_type=jnp.float32)  38.2 us
    select_n x2, other arithmetic, on_device(): row_cache = jnp.take(weights, recv_keys // tok_rows, axis=0)  33.5 us
    scatter x1, local copies, waits for them, and re-layouts, bucket_lists(): jnp.zeros(owners * capacity, jnp.bfloat16).at[slot_index]  28.6 us
  transfers between devices with their start and end apart: 13, of which 9 were waited for; matrix products, arithmetic and copies ran while one was open for 3% of the time, Pallas kernels for 0%

profile of v1, /device:TPU:0, one launch (start us, length us, event | category | flops | bytes accessed | tf_op | source)
XLA Modules:
  0.0 977.8 jit_solution(5083424700576341078)
XLA Ops:
  9.1 5.8 sort.17
  14.9 23.0 %gather_fusion = s32[4096]{0:T(1024)S(1)} fusion(s32[4096]{0:T(1024)S(1)} %add_select_fusion.3, s32[4096]{0:T(1024)S(1)} %get-tuple-element.481), kind=kCustom, calls=%fused_computation | custom fusion | bytes 49152 | tf_op jit(solution)/shard_map/gather | solution.py:59
  43.0 15.5 %scatter_custom_fusion = s32[4096]{0:T(1024)S(1)} fusion(s32[4096]{0:T(1024)S(1)} %get-tuple-element.482, s32[4096]{0:T(1024)S(1)} %select_subtract_fusion, s32[]{:T(128)} %constant.283.clone.1), kind=kCustom, calls=%fused_computation.106 | custom fusion | bytes 16388 | tf_op jit(solution)/shard_map/scatter | solution.py:60
  59.4 28.6 %scatter_custom_fusion.2 = bf16[6144]{0:T(1024)(128)(2,1)S(1)} fusion(s32[4096]{0:T(1024)S(1)} %get-tuple-element.475, bf16[4096]{0:T(1024)(128)(2,1)S(1)} %reshape.307, bf16[]{:T(256)} %constant.298.clone.1), kind=kCustom, calls=%fused_computation.108 | custom fusion | bytes 12290 | tf_op jit(solution)/shard_map/scatter | solution.py:66
  89.9 7.3 all-to-all-start.1
  97.1 16.1 %scatter_custom_fusion.1 = s32[6144]{0:T(1024)} fusion(s32[4096]{0:T(1024)S(1)} %get-tuple-element.475, s32[4096]{0:T(1024)S(1)} %get-tuple-element.480, s32[]{:T(128)} %constant.283.clone.1), kind=kCustom, calls=%fused_computation.101 | custom fusion | bytes 24580 | tf_op jit(solution)/shard_map/scatter | solution.py:63
  113.2 6.0 all-to-all-start
  120.1 5.8 all-to-all-done
  126.0 262.1 %gather_fusion.1 = bf16[6144,4096]{1,0:T(8,128)(2,1)} fusion(bf16[4096,4096]{1,0:T(8,128)(2,1)} %bitcast.101, s32[6144]{0:T(1024)S(1)} %broadcast_clamp_fusion), kind=kCustom, calls=%fused_computation.1 | custom fusion | bytes 100687872 | tf_op jit(solution)/shard_map/jit(_take)/gather | solution.py:104
  388.1 33.4 %broadcast_select_fusion.2 = bf16[8,768,4096]{2,1,0:T(8,128)(2,1)} fusion(bf16[8,768,4096]{2,1,0:T(8,128)(2,1)} %bitcast.102, pred[8,768]{1,0:T(8,128)(4,1)S(1)} %compare_and_fusion), kind=kLoop, calls=%fused_computation.46 | loop fusion | flops 25165824 | bytes 100669440 | tf_op jit(solution)/shard_map/jit(_take)/select_n | solution.py:104
  421.5 44.3 %while.56 = (s32[]{:T(128)}, bf16[8,128,4096]{2,1,0:T(8,128)(2,1)}, s32[8,768]{1,0:T(8,128)S(1)}, bf16[8,768]{1,0:T(8,128)(2,1)}, bf16[8,768,4096]{2,1,0:T(8,128)(2,1)}, /*index=5*/s32[]{:T(128)}) while((s32[]{:T(128)}, bf16[8,128,4096]{2,1,0:T(8,128)(2,1)}, s32[8,768]{1,0:T(8,128)S(1)}, bf16[8,768]{1,0:T(8,128)(2,1)}, ...), condition=%wide.region_7.8_spmd, body=%wide.region_6.7_spmd.sunk | while | flops 805511424 | bytes 8403533 | solution.py:111
  465.9 159.1 %reduce-scatter.2.cloned.1.call-done = bf16[128,4096]{1,0:T(8,128)(2,1)} async-done(((bf16[1024,4096]{1,0:T(8,128)(2,1)}), bf16[128,4096]{1,0:T(8,128)(2,1)}) %reduce-scatter.2.cloned.1.call-update) | async-done | bytes 1048592 | tf_op jit(solution)/shard_map/reduce_scatter | solution.py:112
  625.1 5.2 all-gather.3
  630.3 29.8 %all-gather.7.cloned.1.call-done = bf16[512,4096]{1,0:T(8,128)(2,1)} async-done(((bf16[128,4096]{1,0:T(8,128)(2,1)}), bf16[512,4096]{1,0:T(8,128)(2,1)}) %all-gather.7.cloned.1.call-update) | async-done | bytes 4194320 | tf_op jit(solution)/shard_map/all_gather | solution.py:26
  660.1 10.5 %while.58 = (s32[]{:T(128)}, f32[1,4096]{1,0:T(1,128)S(1)}, f32[128,4096]{1,0:T(8,128)S(1)}, s32[]{:T(128)}, bf16[4,1,4096]{2,1,0:T(2,128)(2,1)S(1)}, /*index=5*/bf16[4,128,4096]{2,1,0:T(8,128)(2,1)}, s32[]{:T(128)}, s32[]{:T(128)}) while((s32[]{:T(128)}, f32[1,4096]{1,0:T(1,128)S(1)}, f32[128,4096]{1,0:T(8,128)S(1)}, ...), condition=%wide.region_10.11_spmd.clone, body=%wide.region_9.10_spmd.clone.sunk | while | flops 2637828 | bytes 5316723 | solution.py:44
  674.6 34.6 %all-gather.9.cloned.1.call-done = bf16[512,4096]{1,0:T(8,128)(2,1)} async-done(((bf16[128,4096]{1,0:T(8,128)(2,1)}), bf16[512,4096]{1,0:T(8,128)(2,1)}) %all-gather.9.cloned.1.call-update) | async-done | bytes 4194320 | tf_op jit(solution)/shard_map/all_gather | solution.py:26
  709.2 10.4 %while.59 = (s32[]{:T(128)}, f32[128,4096]{1,0:T(8,128)S(1)}, s32[]{:T(128)}, bf16[4,1,4096]{2,1,0:T(2,128)(2,1)S(1)}, bf16[4,128,4096]{2,1,0:T(8,128)(2,1)}, /*index=5*/s32[]{:T(128)}, s32[]{:T(128)}, s32[]{:T(128)}, s32[]{:T(128)}) while((s32[]{:T(128)}, f32[128,4096]{1,0:T(8,128)S(1)}, s32[]{:T(128)}, ...), condition=%wide.region_12.13_spmd.clone, body=%wide.region_11.12_spmd.clone.sunk | while | flops 2625544 | bytes 5284007 | solution.py:44
  729.9 42.1 %collective-permute-done = bf16[128,4096]{1,0:T(8,128)(2,1)} collective-permute-done((bf16[128,4096]{1,0:T(8,128)(2,1)S(1)}, bf16[128,4096]{1,0:T(8,128)(2,1)}, u32[]{:S(2)}, u32[]{:S(2)}) %collective-permute-start) | collective-permute-done | bytes 1048608 | tf_op jit(solution)/shard_map/ppermute | solution.py:13
  777.3 42.0 %collective-permute-done.2 = bf16[128,4096]{1,0:T(8,128)(2,1)S(1)} collective-permute-done((bf16[128,4096]{1,0:T(8,128)(2,1)}, bf16[128,4096]{1,0:T(8,128)(2,1)S(1)}, u32[]{:S(2)}, u32[]{:S(2)}) %collective-permute-start.2) | collective-permute-done | bytes 1048608 | tf_op jit(solution)/shard_map/ppermute | solution.py:13
  828.9 36.9 %collective-permute-done.4 = bf16[128,4096]{1,0:T(8,128)(2,1)S(1)} collective-permute-done((bf16[128,4096]{1,0:T(8,128)(2,1)S(1)}, bf16[128,4096]{1,0:T(8,128)(2,1)S(1)}, u32[]{:S(2)}, u32[]{:S(2)}) %collective-permute-start.4) | collective-permute-done | bytes 1048608 | tf_op jit(solution)/shard_map/ppermute | solution.py:13
  871.4 20.2 %collective-permute-done.6 = bf16[128,4096]{1,0:T(8,128)(2,1)S(1)} collective-permute-done((bf16[128,4096]{1,0:T(8,128)(2,1)S(1)}, bf16[128,4096]{1,0:T(8,128)(2,1)S(1)}, u32[]{:S(2)}, u32[]{:S(2)}) %collective-permute-start.6) | collective-permute-done | bytes 1048608 | tf_op jit(solution)/shard_map/ppermute | solution.py:13
  892.7 44.2 %while.57 = (s32[]{:T(128)}, f32[8,768]{1,0:T(8,128)S(1)}, s32[8,768]{1,0:T(8,128)S(1)}, bf16[8,128,4096]{2,1,0:T(8,128)(2,1)}, bf16[8,768,4096]{2,1,0:T(8,128)(2,1)}, /*index=5*/s32[]{:T(128)}, s32[]{:T(128)}) while((s32[]{:T(128)}, f32[8,768]{1,0:T(8,128)S(1)}, s32[8,768]{1,0:T(8,128)S(1)}, bf16[8,128,4096]{2,1,0:T(8,128)(2,1)}, ...), condition=%wide.region_15.16_spmd, body=%wide.region_13.15_spmd.sunk | while | flops 805608960 | bytes 7365717 | solution.py:135
  892.8 5.5 fusion.67
  898.4 5.3 fusion.67
  903.9 5.3 fusion.67
  909.4 5.3 fusion.67
  914.9 5.3 fusion.67
  920.4 5.3 fusion.67
  925.9 5.3 fusion.67
  931.4 5.3 fusion.67
  942.0 5.5 all-to-all-done.2
  947.4 23.0 %gather_fusion.2 = f32[4096]{0:T(1024)S(1)} fusion(f32[6144]{0:T(1024)S(1)} %bitcast.100, s32[4096]{0:T(1024)S(1)} %copy-done.8), kind=kCustom, calls=%fused_computation.2 | custom fusion | bytes 49152 | tf_op jit(solution)/shard_map/jit(_take)/gather | solution.py:137
  (148 shorter events, 118.4 us)
Async XLA Ops:
  14.9 44.3 %copy-start.9 = (bf16[1,128,32]{1,2,0:T(8,128)(2,1)S(1)}, bf16[1,128,32]{1,2,0:T(8,128)(2,1)}, u32[]{:S(2)}) copy-start(bf16[1,128,32]{1,2,0:T(8,128)(2,1)} %param.14) | copy-start | bytes 24580
  59.2 60.3 %copy-start.6 = (s32[4096]{0:T(1024)}, s32[4096]{0:T(1024)S(1)}, u32[]{:S(2)}) copy-start(s32[4096]{0:T(1024)S(1)} %get-tuple-element.475) | copy-start | bytes 49156
  89.9 23.4 %all-to-all-start.1 = ((bf16[8,2,384]{2,1,0:T(2,128)(2,1)}), bf16[8,2,384]{2,1,0:T(2,128)(2,1)S(1)}, u32[]{:S(2)}, u32[]{:S(2)}) async-start(bf16[8,2,384]{2,1,0:T(2,128)(2,1)} %reshape.367), calls=%async_computation.1 | async-start | bytes 24576 | tf_op jit(solution)/shard_map/all_to_all | solution.py:102
  113.2 12.6 %all-to-all-start = ((s32[8,1,768]{2,1,0:T(1,128)}), s32[8,1,768]{2,1,0:T(1,128)S(1)}, u32[]{:S(2)}, u32[]{:S(2)}) async-start(s32[8,1,768]{2,1,0:T(1,128)} %bitcast.18), calls=%async_computation | async-start | bytes 49152 | tf_op jit(solution)/shard_map/all_to_all | solution.py:101
  119.2 505.7 %reduce-scatter.2.cloned.1.call-start = ((), (), s32[]{:S(2)}) async-start(), calls=%async_computation.4 | async-start | bytes 9437184 | tf_op jit(solution)/shard_map/reduce_scatter | solution.py:112
  465.8 159.2 %copy-start.5 = (f32[1,4096]{1,0:T(1,128)S(1)}, f32[1,4096]{1,0:T(1,128)}, u32[]{:S(2)}) copy-start(f32[1,4096]{1,0:T(1,128)} %param.17) | copy-start | bytes 49156
  465.8 194.2 %all-gather.7.cloned.1.call-start = ((), (), s32[]{:S(2)}) async-start(), calls=%async_computation.5 | async-start | bytes 5242880 | tf_op jit(solution)/shard_map/all_gather | solution.py:26
  625.0 84.2 %all-gather.9.cloned.1.call-start = ((), (), s32[]{:S(2)}) async-start(), calls=%async_computation.6 | async-start | bytes 5242880 | tf_op jit(solution)/shard_map/all_gather | solution.py:26
  660.1 10.6 %copy-start.3 = (bf16[128,4096]{1,0:T(8,128)(2,1)S(1)}, bf16[128,4096]{1,0:T(8,128)(2,1)}, u32[]{:S(2)}) copy-start(bf16[128,4096]{1,0:T(8,128)(2,1)} %reduce-scatter.2.cloned.1.call-done) | copy-start | bytes 3145732
  719.6 1.6 copy-start.1
  719.6 1.8 copy-start.4
  722.0 3.2 copy-start
  725.2 46.8 %collective-permute-start = (bf16[128,4096]{1,0:T(8,128)(2,1)S(1)}, bf16[128,4096]{1,0:T(8,128)(2,1)}, u32[]{:S(2)}, u32[]{:S(2)}) collective-permute-start(bf16[128,4096]{1,0:T(8,128)(2,1)S(1)} %get-tuple-element.477), channel_id=1, source_target_pairs={{0,1},{1,2},{2,3},{3,4},{4,5},{5,6},{6,7},{7,0},{8,9},{9,10},{10,1... | collective-permute-start | bytes 3145736 | tf_op jit(solution)/shard_map/ppermute | solution.py:13
  726.6 47.9 %collective-permute-start.1 = (bf16[128,4096]{1,0:T(8,128)(2,1)S(1)}, bf16[128,4096]{1,0:T(8,128)(2,1)S(1)}, u32[]{:S(2)}, u32[]{:S(2)}) collective-permute-start(bf16[128,4096]{1,0:T(8,128)(2,1)S(1)} %get-tuple-element.477), channel_id=1, source_target_pairs={{0,7},{1,0},{2,1},{3,2},{4,3},{5,4},{6,5},{7,6},{8,15},{9,8},{10,9... | collective-permute-start | bytes 3145736 | tf_op jit(solution)/shard_map/ppermute | solution.py:16
  771.9 47.4 %collective-permute-start.2 = (bf16[128,4096]{1,0:T(8,128)(2,1)}, bf16[128,4096]{1,0:T(8,128)(2,1)S(1)}, u32[]{:S(2)}, u32[]{:S(2)}) collective-permute-start(bf16[128,4096]{1,0:T(8,128)(2,1)} %collective-permute-done), channel_id=1, source_target_pairs={{0,1},{1,2},{2,3},{3,4},{4,5},{5,6},{6,7},{7,0},{8,9},{9,10},{10,1... | collective-permute-start | bytes 3145736 | tf_op jit(solution)/shard_map/ppermute | solution.py:13
  774.5 50.5 %collective-permute-start.3 = (bf16[128,4096]{1,0:T(8,128)(2,1)S(1)}, bf16[128,4096]{1,0:T(8,128)(2,1)S(1)}, u32[]{:S(2)}, u32[]{:S(2)}) collective-permute-start(bf16[128,4096]{1,0:T(8,128)(2,1)S(1)} %collective-permute-done.1), channel_id=1, source_target_pairs={{0,7},{1,0},{2,1},{3,2},{4,3},{5,4},{6,5},{7,6},{8,15},{9,8},{10,9... | collective-permute-start | bytes 3145736 | tf_op jit(solution)/shard_map/ppermute | solution.py:16
  819.3 46.5 %collective-permute-start.4 = (bf16[128,4096]{1,0:T(8,128)(2,1)S(1)}, bf16[128,4096]{1,0:T(8,128)(2,1)S(1)}, u32[]{:S(2)}, u32[]{:S(2)}) collective-permute-start(bf16[128,4096]{1,0:T(8,128)(2,1)S(1)} %collective-permute-done.2), channel_id=1, source_target_pairs={{0,1},{1,2},{2,3},{3,4},{4,5},{5,6},{6,7},{7,0},{8,9},{9,10},{10,1... | collective-permute-start | bytes 3145736 | tf_op jit(solution)/shard_map/ppermute | solution.py:13
  825.1 45.3 %collective-permute-start.5 = (bf16[128,4096]{1,0:T(8,128)(2,1)S(1)}, bf16[128,4096]{1,0:T(8,128)(2,1)S(1)}, u32[]{:S(2)}, u32[]{:S(2)}) collective-permute-start(bf16[128,4096]{1,0:T(8,128)(2,1)S(1)} %collective-permute-done.3), channel_id=1, source_target_pairs={{0,7},{1,0},{2,1},{3,2},{4,3},{5,4},{6,5},{7,6},{8,15},{9,8},{10,9... | collective-permute-start | bytes 3145736 | tf_op jit(solution)/shard_map/ppermute | solution.py:16
  865.8 25.9 %collective-permute-start.6 = (bf16[128,4096]{1,0:T(8,128)(2,1)S(1)}, bf16[128,4096]{1,0:T(8,128)(2,1)S(1)}, u32[]{:S(2)}, u32[]{:S(2)}) collective-permute-start(bf16[128,4096]{1,0:T(8,128)(2,1)S(1)} %collective-permute-done.4), channel_id=1, source_target_pairs={{0,1},{1,2},{2,3},{3,4},{4,5},{5,6},{6,7},{7,0},{8,9},{9,10},{10,1... | collective-permute-start | bytes 3145736 | tf_op jit(solution)/shard_map/ppermute | solution.py:13
  892.7 48.1 %copy-start.2 = (f32[128,4096]{1,0:T(8,128)S(1)}, f32[128,4096]{1,0:T(8,128)}, u32[]{:S(2)}) copy-start(f32[128,4096]{1,0:T(8,128)} %get-tuple-element.479) | copy-start | bytes 6291460
  892.7 54.7 %copy-start.8 = (s32[4096]{0:T(1024)S(1)}, s32[4096]{0:T(1024)}, u32[]{:S(2)}) copy-start(s32[4096]{0:T(1024)} %get-tuple-element.474) | copy-start | bytes 49156
  937.5 9.9 %all-to-all-start.2 = ((f32[8,1,768]{2,1,0:T(1,128)}), f32[8,1,768]{2,1,0:T(1,128)S(1)}, u32[]{:S(2)}, u32[]{:S(2)}) async-start(f32[8,1,768]{2,1,0:T(1,128)} %all_to_all.31), calls=%async_computation.3 | async-start | bytes 49152 | tf_op jit(solution)/shard_map/all_to_all | solution.py:136
  947.4 23.0 %copy-start.7 = (s32[4096]{0:T(1024)S(1)}, s32[4096]{0:T(1024)}, u32[]{:S(2)}) copy-start(s32[4096]{0:T(1024)} %copy-done.6) | copy-start | bytes 49156
Sparse Core Ops, SparseCore 0:
  466.0 158.9 reduce-scatter.1
  626.6 33.4 all-gather.6
  674.7 34.4 all-gather.8
